TPU v7x, 256 devices: a whole 4x4x8 slice. The times are simulated.
256 devices in a mesh: section: 2 (over x_hi), ctx: 32 (over z, x_lo, core), mp: 4 (over y).
Axes of the slice: x: 4 (x_hi: 2, x_lo: 2; x = x_hi * 2 + x_lo), y: 4, z: 8, core: 2. Of those that a mesh axis runs over, the one named last changes fastest.
Arguments:
- queries: bfloat16 [2, 8192, 4096], P('section', 'ctx', 'mp'), may hold values from -130 to 130
- keys: bfloat16 [2, 8192, 512], P('section', 'ctx', 'mp'), may hold values from -4.5 to 4.5
- values: bfloat16 [2, 8192, 512], P('section', 'ctx', 'mp'), may hold values from -6 to 6
- doc_lengths: int32 [2, 16], P('section'), may hold values from 1 to 4096, 8192 in all within a row
Outputs:
- attended: bfloat16 [2, 8192, 4096], P('section', ('ctx', 'mp'))
- passed: bfloat16 [2, 8192, 4096], P('section', ('ctx', 'mp'))
All inputs are finite; a program needn't handle non-finite values.
Results may differ from a plain program's by a relative error of at most 0.004.
Values may be sent and summed in bfloat16 or wider, within the bound.
No kernel may reach another device: no remote copies, remote signals or barrier semaphores. Data moves between devices by JAX's collectives and lax.ppermute only.
A program may use at most 192 MiB of HBM per device.

v0:
```python
import math
import jax
import jax.numpy as jnp
from jax import lax
from jax.sharding import PartitionSpec as P

DH = 128
DOCS = 16


def from_behind(block, axis, distance):
    devices = range(lax.axis_size(axis))
    route = [((i - distance) % len(devices), i) for i in devices]
    return lax.ppermute(block, axis, route)


def doc_of(positions, ends):
    return jnp.sum((positions[:, None] >= ends[None, :]).astype(jnp.int32), axis=1)


def body(queries, keys, values, doc_lengths):
    query_rows = queries[0]
    key_rows = keys[0]
    value_rows = values[0]
    lengths = doc_lengths[0]
    rows = query_rows.shape[0]
    kv_heads = key_rows.shape[1] // DH
    heads = query_rows.shape[1] // DH
    group = heads // kv_heads
    cycle = lax.axis_size("ctx")
    base_len = rows * cycle // 16
    position = lax.axis_index("ctx")
    first = position * rows
    ends = jnp.cumsum(lengths)
    query_pos = first + jnp.arange(rows, dtype=jnp.int32)
    query_doc = doc_of(query_pos, ends)
    lookup = query_doc[:, None] == jnp.arange(DOCS, dtype=jnp.int32)[None, :]
    query_len = jnp.sum(jnp.where(lookup, lengths[None, :], 0), axis=1).astype(jnp.float32)
    factor = jnp.maximum(1.0, jnp.log(query_len) / math.log(float(base_len))) * (
        1.0 / math.sqrt(DH)
    )
    query_heads = query_rows.reshape(rows, kv_heads, group, DH)
    key_piece = lax.all_gather(key_rows, "ctx", axis=0, tiled=True)
    value_piece = lax.all_gather(value_rows, "ctx", axis=0, tiled=True)
    top = jnp.full((kv_heads, group, rows), -1e30, jnp.float32)
    count = key_piece.shape[0]
    key_pos = jnp.arange(count, dtype=jnp.int32)
    key_doc = doc_of(key_pos, ends)
    score = jnp.einsum(
        "qhgd,khd->hgqk",
        query_heads,
        key_piece.reshape(count, kv_heads, DH),
        preferred_element_type=jnp.float32,
    )
    score = score * factor[None, None, :, None]
    allowed = (
        (query_doc[:, None] == key_doc[None, :])
        & (key_pos[None, :] <= query_pos[:, None])
        & (key_pos[None, :] >= 0)
    )
    score = jnp.where(allowed[None, None], score, -1e30)
    new_top = jnp.maximum(top, jnp.max(score, axis=-1))
    weight = jnp.where(allowed[None, None], jnp.exp(score - new_top[..., None]), 0.0)
    total = jnp.sum(weight, axis=-1)
    update = jnp.einsum(
        "hgqk,khd->qhgd",
        weight.astype(jnp.bfloat16),
        value_piece.reshape(count, kv_heads, DH),
        preferred_element_type=jnp.float32,
    )
    summed = update
    top, total, summed = (new_top, total, summed)
    result = summed / jnp.transpose(total, (2, 0, 1))[..., None]
    result = result.astype(jnp.bfloat16).reshape(rows, heads * DH)
    own = lax.all_to_all(result, "mp", split_axis=0, concat_axis=1, tiled=True)
    moved = from_behind(own, "section", 1)
    return (own[None], moved[None])


def solution(mesh):
    return jax.shard_map(
        body,
        mesh=mesh,
        in_specs=(
            P("section", "ctx", "mp"),
            P("section", "ctx", "mp"),
            P("section", "ctx", "mp"),
            P("section", None),
        ),
        out_specs=(P("section", ("ctx", "mp"), None), P("section", ("ctx", "mp"), None)),
        check_vma=False,
    )
```

profile of v0, /device:TPU:4, one launch (start us, length us, event | category | flops | bytes accessed | tf_op | source)
XLA Modules:
  0.0 209.2 jit_solution(6878893363365230713)
XLA Ops:
  7.2 0.0 all-gather.5.cloned.1.call-start
  7.2 0.7 all-gather.5.cloned.1.call-update
  7.9 0.0 all-gather.7.cloned.1.call-start
  7.9 0.7 all-gather.7.cloned.1.call-update
  8.7 0.7 copy.19
  9.4 0.1 reduce.2
  9.5 0.2 convert_reduce_fusion
  9.7 0.1 convert_reduce_fusion.1
  9.8 3.7 %fusion.7 = pred[256,8192]{0,1:T(8,128)(4,1)S(1)} fusion(s32[256]{0:T(256)S(1)} %iota_add_fusion, s32[256]{0:T(256)S(1)} %convert_reduce_fusion.1, s32[8192]{0:T(1024)S(1)} %convert_reduce_fusion), kind=kLoop, calls=%fused_computation.10 | loop fusion | flops 6291456 | bytes 2131968 | tf_op jit(solution)/shard_map/and | solution.py:57
  13.5 0.7 select_reduce_fusion
  14.3 1.1 copy.27
  15.4 61.5 %all-gather.5.cloned.1.call-done = bf16[1,8192,128]{2,1,0:T(8,128)(2,1)} async-done(((bf16[1,256,128]{2,1,0:T(8,128)(2,1)}), bf16[1,8192,128]{2,1,0:T(8,128)(2,1)}) %all-gather.5.cloned.1.call-update) | async-done | bytes 2097168 | tf_op jit(solution)/shard_map/all_gather | solution.py:43
  76.9 24.9 %fusion = (f32[8,256]{1,0:T(8,128)S(1)}, f32[8192,256,8]{1,0,2:T(8,128)}) fusion(f32[256]{0:T(256)S(1)} %maximum_multiply_fusion, pred[256,8192]{0,1:T(8,128)(4,1)S(1)} %fusion.7, bf16[256,8,128]{2,1,0:T(8,128)(2,1)S(1)} %bitcast.88, bf16[1,8192,128]{2,1,0:T(8,128)(2,1)} %all-gather.5.cloned.1.call-done), kind=kOutput, calls=%fused_computation.3 | convolution fusion | flops 4345296896 | bytes 71836672 | tf_op jit(solution)/shard_map/qhgd,khd->hgqk/dot_general | solution.py:49
  101.8 21.9 %fusion.1 = f32[8,256]{1,0:T(8,128)S(1)} fusion(f32[8192,256,8]{1,0,2:T(8,128)} %get-tuple-element.3, f32[8,256]{1,0:T(8,128)S(1)} %broadcast_maximum_fusion, f32[256]{0:T(256)S(1)} %maximum_multiply_fusion, pred[256,8192]{0,1:T(8,128)(4,1)S(1)} %fusion.7), kind=kLoop, calls=%fused_computation.4 | loop fusion | flops 83884032 | bytes 69223424 | tf_op jit(solution)/shard_map/reduce_sum | solution.py:64
  123.7 19.1 %all-gather.7.cloned.1.call-done = bf16[1,8192,128]{2,1,0:T(8,128)(2,1)} async-done(((bf16[1,256,128]{2,1,0:T(8,128)(2,1)}), bf16[1,8192,128]{2,1,0:T(8,128)(2,1)}) %all-gather.7.cloned.1.call-update) | async-done | bytes 2097168 | tf_op jit(solution)/shard_map/all_gather | solution.py:44
  142.8 29.6 %divide_convert_fusion = bf16[256,1,8,128]{3,0,2,1:T(8,128)(2,1)S(1)} fusion(bf16[1,8192,128]{2,1,0:T(8,128)(2,1)} %all-gather.7.cloned.1.call-done, f32[8192,256,8]{1,0,2:T(8,128)} %get-tuple-element.3, f32[8,256]{1,0:T(8,128)S(1)} %broadcast_maximum_fusion, f32[256]{0:T(256)S(1)} %maximum_multiply_fusion, pred[256,8192]{0,1:T(8,128)(4,1)S(1)} %fusion.7, ...), kind=kOutput, calls=%fused_computation.15 | convolution fusion | flops 4379377664 | bytes 71844864 | tf_op jit(solution)/shard_map/hgqk,khd->qhgd/dot_general | solution.py:65
  172.4 0.3 copy.22
  172.8 0.2 all_to_all.14
  173.0 14.0 %all_to_all.19 = bf16[4,64,1024]{2,1,0:T(8,128)(2,1)S(1)} all-to-all(bf16[4,64,1024]{2,1,0:T(8,128)(2,1)S(1)} %all_to_all.14), channel_id=1, replica_groups=mesh['section'=2,'ctx'=32,'mp'=4] {'mp'}, dimensions={0} | all-to-all | bytes 1048576 | tf_op jit(solution)/shard_map/all_to_all | solution.py:75
  187.0 0.9 collective-permute-start
  187.9 0.4 copy.23
  188.3 1.2 broadcast_in_dim.64
  189.5 12.0 %collective-permute-done = bf16[64,4096]{1,0:T(8,128)(2,1)S(1)} collective-permute-done((bf16[64,4096]{1,0:T(8,128)(2,1)S(1)}, bf16[64,4096]{1,0:T(8,128)(2,1)S(1)}, u32[]{:S(2)}, u32[]{:S(2)}) %collective-permute-start) | collective-permute-done | bytes 524320 | tf_op jit(solution)/shard_map/ppermute | solution.py:14
  201.5 0.8 copy.33
  (5 shorter events, 0.1 us)
Async XLA Ops:
  7.2 69.7 %all-gather.5.cloned.1.call-start = ((), (), s32[]{:S(2)}) async-start(), calls=%async_computation.1 | async-start | bytes 2162688 | tf_op jit(solution)/shard_map/all_gather | solution.py:43
  7.9 134.9 %all-gather.7.cloned.1.call-start = ((), (), s32[]{:S(2)}) async-start(), calls=%async_computation.2 | async-start | bytes 2162688 | tf_op jit(solution)/shard_map/all_gather | solution.py:44
  187.0 14.5 %collective-permute-start = (bf16[64,4096]{1,0:T(8,128)(2,1)S(1)}, bf16[64,4096]{1,0:T(8,128)(2,1)S(1)}, u32[]{:S(2)}, u32[]{:S(2)}) collective-permute-start(bf16[64,4096]{1,0:T(8,128)(2,1)S(1)} %bitcast.87), channel_id=1, source_target_pairs={{128,0},{0,128},{129,1},{1,129},{130,2},{2,130},{131,3},{3,131},{1... | collective-permute-start | bytes 1572872 | tf_op jit(solution)/shard_map/ppermute | solution.py:14
Sparse Core Ops, SparseCore 0:
  9.8 67.0 all-gather.4
  78.8 63.9 all-gather.6
where the time goes:
time: 209 us
  waiting for transfers between devices  93.9 us (45%)
  matrix products  54.5 us (26%)
  other arithmetic  26.8 us (13%)
  between operations  14.1 us (7%)
  blocking collectives  14 us (7%)
  local copies, waits for them, and re-layouts  4.85 us (2%)
    all_gather x1, waiting for transfers between devices, body(): key_piece = lax.all_gather(key_rows, 'ctx', axis=0, tiled=True)  61.5 us
    dot_general x1, matrix products, body(): jnp.einsum('hgqk,khd->qhgd', weight.astype(jnp.bfloat16), value_piece.res...  29.6 us
    dot_general x1, matrix products, body(): jnp.einsum('qhgd,khd->hgqk', query_heads, key_piece.reshape(count, kv_hea...  24.9 us
    reduce_sum x1, other arithmetic, body(): total = jnp.sum(weight, axis=-1)  21.9 us
    all_gather x1, waiting for transfers between devices, body(): value_piece = lax.all_gather(value_rows, 'ctx', axis=0, tiled=True)  19.1 us
    all_to_all x1, blocking collectives, body(): own = lax.all_to_all(result, 'mp', split_axis=0, concat_axis=1, tiled=True)  14 us
    ppermute x1, waiting for transfers between devices, from_behind(): return lax.ppermute(block, axis, route)  12 us
  transfers between devices with their start and end apart: 3, of which 3 were waited for; matrix products, arithmetic and copies ran while one was open for 26% of the time, Pallas kernels for 0%

commit v1 on v0

--- a/solution.py
+++ b/solution.py
@@ -3,6 +3,7 @@
 import jax.numpy as jnp
 from jax import lax
 from jax.sharding import PartitionSpec as P
+from jax.lax import all_to_all, psum
 
 DH = 128
 DOCS = 16
@@ -40,7 +41,19 @@
         1.0 / math.sqrt(DH)
     )
     query_heads = query_rows.reshape(rows, kv_heads, group, DH)
-    key_piece = lax.all_gather(key_rows, "ctx", axis=0, tiled=True)
+
+    def vector_derive(raw):
+        return jnp.concatenate(
+            all_to_all(
+                jnp.stack([raw] * psum(1, axis_name="ctx"), axis=0),
+                "ctx",
+                split_axis=0,
+                concat_axis=0,
+            ),
+            axis=0,
+        )
+
+    key_piece = vector_derive(key_rows)
     value_piece = lax.all_gather(value_rows, "ctx", axis=0, tiled=True)
     top = jnp.full((kv_heads, group, rows), -1e30, jnp.float32)
     count = key_piece.shape[0]

time: 209 us -> 191 us (0.914)
  waiting for transfers between devices: 93.9 us -> 62.9 us
  starting transfers between devices: 1 us -> 10.5 us
  local copies, waits for them, and re-layouts: 4.85 us -> 7.51 us
    all_gather x1 -> x0, waiting for transfers between devices: 61.5 us -> none  [body(): key_piece = lax.all_gather(key_rows, 'ctx', axis=0, tiled=True)]
    all_to_all x0 -> x1, waiting for transfers between devices: none -> 50.5 us  [vector_derive(): all_to_all(jnp.stack([raw] * psum(1, axis_name='ctx'), axis=0), 'ctx', sp...]
    all_gather x1, waiting for transfers between devices: 19.1 us -> 0.02 us  [body(): value_piece = lax.all_gather(value_rows, 'ctx', axis=0, tiled=True)]
    all_to_all x0 -> x1, starting transfers between devices: none -> 9.62 us  [vector_derive(): all_to_all(jnp.stack([raw] * psum(1, axis_name='ctx'), axis=0), 'ctx', sp...]
    another operation x1 -> x2, local copies, waits for them, and re-layouts: 0.73 us -> 3.4 us  [the longest x1 2.66 us: vector_derive(): jnp.stack([raw] * psum(1, axis_name='ctx'), axis=0)]
  transfers between devices with their start and end apart: 3 -> 3, of which waited for: 3 -> 2; matrix products, arithmetic and copies ran while one was open for 26% -> 29% of each run, Pallas kernels for 0% -> 0%
where the time goes in v1:
time: 191 us; the launch traced here: 190 us
  waiting for transfers between devices  62.9 us (33%)
  matrix products  54.5 us (29%)
  other arithmetic  26.6 us (14%)
  between operations  14.1 us (7%)
  blocking collectives  14 us (7%)
  starting transfers between devices  10.5 us (5%)
  local copies, waits for them, and re-layouts  7.51 us (4%)
    all_to_all x1, waiting for transfers between devices, vector_derive(): all_to_all(jnp.stack([raw] * psum(1, axis_name='ctx'), axis=0), 'ctx', sp...  50.5 us
    dot_general x1, matrix products, body(): jnp.einsum('hgqk,khd->qhgd', weight.astype(jnp.bfloat16), value_piece.res...  29.7 us
    dot_general x1, matrix products, body(): jnp.einsum('qhgd,khd->hgqk', query_heads, key_piece.reshape(count, kv_hea...  24.8 us
    reduce_sum x1, other arithmetic, body(): total = jnp.sum(weight, axis=-1)  21.7 us
    all_to_all x1, blocking collectives, body(): own = lax.all_to_all(result, 'mp', split_axis=0, concat_axis=1, tiled=True)  14 us
    ppermute x1, waiting for transfers between devices, from_behind(): return lax.ppermute(block, axis, route)  11.6 us
    all_to_all x1, starting transfers between devices, vector_derive(): all_to_all(jnp.stack([raw] * psum(1, axis_name='ctx'), axis=0), 'ctx', sp...  9.62 us
  transfers between devices with their start and end apart: 3, of which 2 were waited for; matrix products, arithmetic and copies ran while one was open for 29% of the time, Pallas kernels for 0%

profile of v1, /device:TPU:4, one launch (start us, length us, event | category | flops | bytes accessed | tf_op | source)
XLA Modules:
  0.0 190.2 jit_solution(7032499518574587754)
XLA Ops:
  7.2 2.7 %stack.3 = bf16[32,256,128]{2,1,0:T(8,128)(2,1)} broadcast(bf16[256,128]{1,0:T(8,128)(2,1)} %bitcast.88), dimensions={1,2} | broadcast | bytes 2162688 | tf_op jit(solution)/shard_map/stack | solution.py:48
  9.8 9.6 %all-to-all-start = ((bf16[32,256,128]{2,1,0:T(8,128)(2,1)}), bf16[32,256,128]{2,1,0:T(8,128)(2,1)}, u32[]{:S(2)}, u32[]{:S(2)}) async-start(bf16[32,256,128]{2,1,0:T(8,128)(2,1)} %stack.3), calls=%async_computation | async-start | bytes 4194304 | tf_op jit(solution)/shard_map/all_to_all | solution.py:47
  19.5 0.0 all-gather.3.cloned.1.call-start
  19.5 0.7 all-gather.3.cloned.1.call-update
  20.2 0.7 copy.19
  21.0 0.1 reduce.2
  21.1 1.1 copy.27
  22.2 0.1 convert_reduce_fusion.1
  22.3 0.7 select_reduce_fusion
  23.1 0.2 convert_reduce_fusion
  23.3 3.7 %fusion.7 = pred[256,8192]{0,1:T(8,128)(4,1)S(1)} fusion(s32[256]{0:T(256)S(1)} %iota_add_fusion, s32[256]{0:T(256)S(1)} %convert_reduce_fusion.1, s32[8192]{0:T(1024)S(1)} %convert_reduce_fusion), kind=kLoop, calls=%fused_computation.10 | loop fusion | flops 6291456 | bytes 2131968 | tf_op jit(solution)/shard_map/and | solution.py:70
  27.0 50.5 %all-to-all-done = bf16[32,256,128]{2,1,0:T(8,128)(2,1)} async-done(((bf16[32,256,128]{2,1,0:T(8,128)(2,1)}), bf16[32,256,128]{2,1,0:T(8,128)(2,1)}, u32[]{:S(2)}, u32[]{:S(2)}) %all-to-all-start) | async-done | bytes 2097184 | tf_op jit(solution)/shard_map/all_to_all | solution.py:47
  77.5 24.8 %fusion = (f32[8,256]{1,0:T(8,128)S(1)}, f32[8192,256,8]{1,0,2:T(8,128)}) fusion(f32[256]{0:T(256)S(1)} %maximum_multiply_fusion, pred[256,8192]{0,1:T(8,128)(4,1)S(1)} %fusion.7, bf16[8192,128,1]{1,0,2:T(8,128)(2,1)} %bitcast.3, bf16[256,8,128]{2,1,0:T(8,128)(2,1)S(1)} %bitcast.85), kind=kOutput, calls=%fused_computation.3 | convolution fusion | flops 4345296896 | bytes 71836672 | tf_op jit(solution)/shard_map/qhgd,khd->hgqk/dot_general | solution.py:62
  102.4 21.7 %fusion.1 = f32[8,256]{1,0:T(8,128)S(1)} fusion(f32[8192,256,8]{1,0,2:T(8,128)} %get-tuple-element.3, f32[8,256]{1,0:T(8,128)S(1)} %broadcast_maximum_fusion, f32[256]{0:T(256)S(1)} %maximum_multiply_fusion, pred[256,8192]{0,1:T(8,128)(4,1)S(1)} %fusion.7), kind=kLoop, calls=%fused_computation.4 | loop fusion | flops 83884032 | bytes 69223424 | tf_op jit(solution)/shard_map/reduce_sum | solution.py:77
  124.1 0.0 all-gather.3.cloned.1.call-done
  124.1 29.7 %divide_convert_fusion = bf16[256,1,8,128]{3,0,2,1:T(8,128)(2,1)S(1)} fusion(bf16[1,8192,128]{2,1,0:T(8,128)(2,1)} %all-gather.3.cloned.1.call-done, f32[8192,256,8]{1,0,2:T(8,128)} %get-tuple-element.3, f32[8,256]{1,0:T(8,128)S(1)} %broadcast_maximum_fusion, f32[256]{0:T(256)S(1)} %maximum_multiply_fusion, pred[256,8192]{0,1:T(8,128)(4,1)S(1)} %fusion.7, ...), kind=kOutput, calls=%fused_computation.13 | convolution fusion | flops 4379377664 | bytes 71844864 | tf_op jit(solution)/shard_map/hgqk,khd->qhgd/dot_general | solution.py:78
  153.8 0.3 copy.22
  154.2 0.2 all_to_all.18
  154.4 14.0 %all_to_all.24 = bf16[4,64,1024]{2,1,0:T(8,128)(2,1)S(1)} all-to-all(bf16[4,64,1024]{2,1,0:T(8,128)(2,1)S(1)} %all_to_all.18), channel_id=1, replica_groups=mesh['section'=2,'ctx'=32,'mp'=4] {'mp'}, dimensions={0} | all-to-all | bytes 1048576 | tf_op jit(solution)/shard_map/all_to_all | solution.py:88
  168.5 0.8 collective-permute-start
  169.3 0.4 copy.23
  169.7 1.2 broadcast_in_dim.64
  170.9 11.6 %collective-permute-done = bf16[64,4096]{1,0:T(8,128)(2,1)S(1)} collective-permute-done((bf16[64,4096]{1,0:T(8,128)(2,1)S(1)}, bf16[64,4096]{1,0:T(8,128)(2,1)S(1)}, u32[]{:S(2)}, u32[]{:S(2)}) %collective-permute-start) | collective-permute-done | bytes 524320 | tf_op jit(solution)/shard_map/ppermute | solution.py:15
  182.5 0.8 copy.33
  (5 shorter events, 0.1 us)
Async XLA Ops:
  9.8 67.7 %all-to-all-start = ((bf16[32,256,128]{2,1,0:T(8,128)(2,1)}), bf16[32,256,128]{2,1,0:T(8,128)(2,1)}, u32[]{:S(2)}, u32[]{:S(2)}) async-start(bf16[32,256,128]{2,1,0:T(8,128)(2,1)} %stack.3), calls=%async_computation | async-start | bytes 4194304 | tf_op jit(solution)/shard_map/all_to_all | solution.py:47
  19.5 104.6 %all-gather.3.cloned.1.call-start = ((), (), s32[]{:S(2)}) async-start(), calls=%async_computation.2 | async-start | bytes 2162688 | tf_op jit(solution)/shard_map/all_gather | solution.py:57
  168.5 14.1 %collective-permute-start = (bf16[64,4096]{1,0:T(8,128)(2,1)S(1)}, bf16[64,4096]{1,0:T(8,128)(2,1)S(1)}, u32[]{:S(2)}, u32[]{:S(2)}) collective-permute-start(bf16[64,4096]{1,0:T(8,128)(2,1)S(1)} %bitcast.87), channel_id=1, source_target_pairs={{128,0},{0,128},{129,1},{1,129},{130,2},{2,130},{131,3},{3,131},{1... | collective-permute-start | bytes 1572872 | tf_op jit(solution)/shard_map/ppermute | solution.py:15
Sparse Core Ops, SparseCore 0:
  22.1 74.4 all-gather.2
